TPU v7x, 256 devices: a whole 4x4x8 slice. The times are simulated.
256 devices in a mesh: dp: 32 (over x_lo, z, core), blk: 8 (over y, x_hi).
Axes of the slice: x: 4 (x_hi: 2, x_lo: 2; x = x_hi * 2 + x_lo), y: 4, z: 8, core: 2. Of those that a mesh axis runs over, the one named last changes fastest.
Arguments:
- inputs: bfloat16 [8, 16384, 4096], P('blk', 'dp'), may hold values from -6 to 6
- out_grads: bfloat16 [8, 16384, 4096], P('blk', 'dp'), may hold values from -8 to 8
- test_matrix: bfloat16 [8, 4096, 256], P('blk'), may hold values from -6 to 6
- momentum: bfloat16 [8, 4096, 4096], P(None, 'blk', 'dp'), may hold values from -6 to 6
Outputs:
- update: bfloat16 [8, 4096, 4096], P(None, 'blk', 'dp')
All inputs are finite; a program needn't handle non-finite values.
Results may differ from a plain program's by a relative error of at most 0.0035.
Values may be sent and summed in bfloat16 or wider, within the bound.
No kernel may reach another device: no remote copies, remote signals or barrier semaphores. Data moves between devices by JAX's collectives and lax.ppermute only.
A program may use at most 128 MiB of HBM per device.

v0:
```python
import jax
import jax.numpy as jnp
from jax import lax
from jax.sharding import Mesh
from jax.sharding import PartitionSpec as P

DP = ("dp_0", "dp_1", "dp_2")


def filled_up(lines, devices):
    spare = -len(lines) % devices
    return jnp.pad(lines, [(0, spare)] + [(0, 0)] * (lines.ndim - 1))


def copy_for_each(x, axis):
    devices = lax.axis_size(axis)
    return lax.all_to_all(jnp.broadcast_to(x[None], (devices, *x.shape)), axis, 0, 0, tiled=True)


def in_order(blocks, dim):
    blocks = jnp.moveaxis(blocks, 0, dim)
    lengths = blocks.shape
    return blocks.reshape(*lengths[:dim], lengths[dim] * lengths[dim + 1], *lengths[dim + 2 :])


def whole_of(x, axes, dim):
    far, near = axes
    first = copy_for_each(x, far)
    blocks = jnp.swapaxes(copy_for_each(first, near), 0, 1)
    return in_order(blocks.reshape(-1, *x.shape), dim)


def in_blocks(x, dim, devices):
    lengths = x.shape
    blocks = x.reshape(*lengths[:dim], devices, lengths[dim] // devices, *lengths[dim + 1 :])
    return jnp.moveaxis(blocks, dim, 0)


def sum_at_owner(x, axis, dim):
    blocks = in_blocks(x, dim, lax.axis_size(axis))
    arrived = lax.all_to_all(blocks, axis, split_axis=0, concat_axis=0, tiled=True)
    return arrived.sum(axis=0)


def sum_by_axis(x, axes, dim):
    far, near = axes
    blocks = in_blocks(x, dim, lax.axis_size(far))
    nearer = sum_at_owner(blocks, near, dim + 1)
    arrived = lax.all_to_all(nearer, far, split_axis=0, concat_axis=0, tiled=True)
    return arrived.sum(axis=0)


def total_of(x, axes):
    lines = x.reshape(-1, x.shape[-1])
    padded = filled_up(lines, lax.axis_size(axes[0]) * lax.axis_size(axes[1]))
    whole = whole_of(sum_by_axis(padded, axes, 0), axes, 0)
    return lax.slice_in_dim(whole, 0, len(lines)).reshape(x.shape)


def collect(x, axis, dim):
    blocks = copy_for_each(x, axis)
    return in_order(blocks, dim)


def total_of_2(x, axes):
    lines = x.reshape(-1, x.shape[-1])
    own = sum_at_owner(filled_up(lines, lax.axis_size(axes)), axes, 0)
    whole = collect(own, axes, 0)
    return whole[: len(lines)].reshape(x.shape)


def inner_gram(columns):
    return lax.dot_general(
        columns, columns, (((0,), (0,)), ((), ())), precision=lax.Precision.HIGHEST
    )


def cholesky_pass(columns, gram_matrix):
    lower_factor = jnp.linalg.cholesky(gram_matrix)
    return lax.linalg.triangular_solve(
        lower_factor, columns, left_side=False, lower=True, transpose_a=True
    )


def shards(inputs, out_grads, test_matrix, momentum):
    features = inputs[0]
    errors = out_grads[0]
    probes = test_matrix[0]
    replicas = lax.axis_size(DP)
    scale = 1.0 / (features.shape[1] * features.shape[0] * replicas)
    projected = jnp.dot(features, probes, preferred_element_type=jnp.float32).astype(jnp.bfloat16)
    token_gram = lax.dot_general(
        errors, errors, (((1,), (1,)), ((), ())), preferred_element_type=jnp.float32
    ).astype(jnp.bfloat16)
    mixed_rows = jnp.dot(token_gram, projected, preferred_element_type=jnp.float32).astype(
        jnp.bfloat16
    )
    sketch_term = (
        lax.dot_general(
            features, mixed_rows, (((0,), (0,)), ((), ())), preferred_element_type=jnp.float32
        )
        * scale
    )
    sketch = total_of(sketch_term, (("dp_0", "dp_1"), "dp_2"))
    basis = cholesky_pass(sketch, inner_gram(sketch)).astype(jnp.bfloat16)
    reduced = jnp.dot(features, basis, preferred_element_type=jnp.float32).astype(jnp.bfloat16)
    shaped = jnp.dot(token_gram, reduced, preferred_element_type=jnp.float32).astype(jnp.bfloat16)
    core_term = (
        lax.dot_general(
            reduced, shaped, (((0,), (0,)), ((), ())), preferred_element_type=jnp.float32
        )
        * scale
    )
    core_matrix = total_of_2(core_term, DP)
    shifted = core_matrix + jnp.eye(core_matrix.shape[0], dtype=jnp.float32)
    lower_factor = jnp.linalg.cholesky(shifted)
    half_solved = lax.linalg.triangular_solve(lower_factor, core_matrix, left_side=True, lower=True)
    factor = lax.linalg.triangular_solve(
        lower_factor, half_solved, left_side=True, lower=True, transpose_a=True
    )
    columns = lax.all_to_all(momentum, "blk", split_axis=0, concat_axis=1, tiled=True)[0]
    coeffs = lax.dot_general(
        basis, columns, (((0,), (0,)), ((), ())), preferred_element_type=jnp.float32
    )
    scaled = jnp.dot(factor, coeffs, precision=lax.Precision.HIGHEST).astype(jnp.bfloat16)
    fresh = (
        columns.astype(jnp.float32) - jnp.dot(basis, scaled, preferred_element_type=jnp.float32)
    ).astype(jnp.bfloat16)
    return lax.all_to_all(fresh[None], "blk", split_axis=1, concat_axis=0, tiled=True)


def solution(mesh):
    torus = Mesh(mesh.devices.reshape(2, 8, 2, mesh.shape["blk"]), ("dp_0", "dp_1", "dp_2", "blk"))
    in_specs = (P("blk", DP, None), P("blk", DP, None), P("blk", None, None), P(None, "blk", DP))
    out_specs = P(None, "blk", DP)
    return jax.shard_map(
        shards, mesh=torus, in_specs=in_specs, out_specs=out_specs, check_vma=False
    )
```

profile of v0, /device:TPU:8, one launch (start us, length us, event | category | flops | bytes accessed | tf_op | source)
XLA Modules:
  0.0 433.2 jit_solution(7566562634158218286)
XLA Ops:
  0.0 6.0 %fusion.16 = bf16[512,512]{1,0:T(8,128)(2,1)S(1)} fusion(bf16[1,512,4096]{2,1,0:T(8,128)(2,1)} %param.6), kind=kOutput, calls=%fused_computation.26 | convolution fusion | flops 2147745792 | bytes 4718592 | tf_op jit(solution)/shard_map/dot_general | solution.py:92
  6.0 1.3 fusion.19
  7.3 5.9 %fusion = f32[4096,256]{0,1:T(8,128)} fusion(bf16[1,512,4096]{2,1,0:T(8,128)(2,1)} %param.5, bf16[512,512]{1,0:T(8,128)(2,1)S(1)} %fusion.16, bf16[512,256]{1,0:T(8,128)(2,1)S(1)} %fusion.19), kind=kOutput, calls=%fused_computation.5 | convolution fusion | flops 1209139200 | bytes 9175040 | tf_op jit(solution)/shard_map/dot_general | solution.py:99
  13.2 6.6 %reshape_reshape.6 = f32[16,2,128,256]{2,1,0,3:T(2,128)} reshape(f32[4096,256]{0,1:T(8,128)} %fusion) | data formatting | bytes 8388608 | tf_op jit(solution)/shard_map/reshape;reshape | solution.py:35
  19.8 4.5 %copy.56 = f32[16,2,128,256]{2,0,3,1:T(8,128)} copy(f32[16,2,128,256]{2,1,0,3:T(2,128)} %reshape_reshape.6) | data formatting | bytes 8388608 | tf_op jit(solution)/shard_map/reshape;reshape | solution.py:35
  24.2 5.6 %all-to-all-start.1 = ((f32[2,16,128,256]{2,1,3,0:T(8,128)}), f32[2,16,128,256]{2,1,3,0:T(8,128)}, u32[]{:S(2)}, u32[]{:S(2)}) async-start(f32[2,16,128,256]{2,1,3,0:T(8,128)} %bitcast.138), calls=%async_computation.1 | async-start | bytes 8388608 | tf_op jit(solution)/shard_map/all_to_all | solution.py:41
  29.9 4.5 %all-to-all-done.1 = f32[2,16,128,256]{2,1,3,0:T(8,128)} async-done(((f32[2,16,128,256]{2,1,3,0:T(8,128)}), f32[2,16,128,256]{2,1,3,0:T(8,128)}, u32[]{:S(2)}, u32[]{:S(2)}) %all-to-all-start.1) | async-done | bytes 4194336 | tf_op jit(solution)/shard_map/all_to_all | solution.py:41
  34.3 2.7 reduce_sum.27
  37.8 58.8 %all_to_all.54 = f32[16,128,256]{1,2,0:T(8,128)S(1)} all-to-all(f32[16,128,256]{1,2,0:T(8,128)S(1)} %copy.30), channel_id=1, replica_groups=mesh['dp_0'=2,'dp_1'=8,'dp_2'=2,'blk'=8] {'dp_0','dp_1'}, dimensions={0} | all-to-all | bytes 4194304 | tf_op jit(solution)/shard_map/all_to_all | solution.py:49
  96.7 1.6 broadcast_in_dim.8
  98.3 4.8 %all-to-all-start.3 = ((f32[16,128,256]{2,1,0:T(8,128)}), f32[16,128,256]{2,1,0:T(8,128)S(1)}, u32[]{:S(2)}, u32[]{:S(2)}) async-start(f32[16,128,256]{2,1,0:T(8,128)} %broadcast_in_dim.8), calls=%async_computation.3 | async-start | bytes 4194304 | tf_op jit(solution)/shard_map/all_to_all | solution.py:17
  103.1 48.9 %all-to-all-done.3 = f32[16,128,256]{2,1,0:T(8,128)S(1)} async-done(((f32[16,128,256]{2,1,0:T(8,128)}), f32[16,128,256]{2,1,0:T(8,128)S(1)}, u32[]{:S(2)}, u32[]{:S(2)}) %all-to-all-start.3) | async-done | bytes 2097184 | tf_op jit(solution)/shard_map/all_to_all | solution.py:17
  152.5 7.1 %all_to_all.51 = f32[2,16,128,256]{3,2,1,0:T(8,128)S(1)} all-to-all(f32[2,16,128,256]{3,2,1,0:T(8,128)S(1)} %broadcast_in_dim.10), channel_id=1, replica_groups=mesh['dp_0'=2,'dp_1'=8,'dp_2'=2,'blk'=8] {'dp_2'}, dimensions={0} | all-to-all | bytes 8388608 | tf_op jit(solution)/shard_map/all_to_all | solution.py:17
  159.6 1.9 copy-done.2
  161.5 6.8 %fusion.28 = f32[256,256]{1,0:T(8,128)S(1)} fusion(f32[2,16,128,256]{3,2,1,0:T(8,128)S(1)} %all_to_all.51), kind=kOutput, calls=%fused_computation.32 | convolution fusion | flops 3221225472 | bytes 4456448 | tf_op jit(solution)/shard_map/dot_general | solution.py:73
  168.5 11.7 %cholesky.130 = f32[128,128]{1,0:T(8,128)S(1)} custom-call(f32[128,128]{1,0:T(8,128)S(1)} %cholesky.194), custom_call_target="Cholesky" | custom-call | tf_op jit(solution)/shard_map/jit(cholesky)/cholesky | solution.py:79
  180.2 10.2 %custom-call.19 = f32[1,128,128]{1,2,0:T(8,128)S(1)} custom-call(f32[1,128,128]{2,1,0:T(8,128)S(1)} %get-tuple-element.49), custom_call_target="InvertDiagBlocksLowerTriangular" | custom-call | tf_op jit(solution)/shard_map/jit(cholesky)/cholesky | solution.py:79
  190.9 11.7 %cholesky.147 = f32[128,128]{1,0:T(8,128)S(1)} custom-call(f32[128,128]{1,0:T(8,128)S(1)} %convolution_subtract_fusion.5), custom_call_target="Cholesky" | custom-call | tf_op jit(solution)/shard_map/jit(cholesky)/cholesky | solution.py:79
  204.8 4.1 while.2
  205.5 1.4 bitcast_dynamic-update-slice_fusion.4
  207.5 1.4 bitcast_dynamic-update-slice_fusion.4
  208.9 19.8 %custom-call.16 = f32[2,128,128]{1,2,0:T(8,128)S(1)} custom-call(f32[2,128,128]{2,1,0:T(8,128)S(1)} %get-tuple-element.13), custom_call_target="InvertDiagBlocksLowerTriangular" | custom-call | tf_op jit(solution)/shard_map/triangular_solve | solution.py:80
  228.8 2.5 copy.33
  231.3 2.0 fusion.61
  233.4 3.5 convolution_subtract_fusion.1
  237.0 2.0 convolution_convert_fusion
  239.0 1.0 copy-done.5
  240.0 1.3 fusion.24
  241.8 19.0 %all_to_all.52 = f32[32,8,256]{2,1,0:T(8,128)S(1)} all-to-all(f32[32,8,256]{2,1,0:T(8,128)S(1)} %fusion.34), channel_id=1, replica_groups=mesh['dp_0'=2,'dp_1'=8,'dp_2'=2,'blk'=8] {'dp_0','dp_1','dp_2'}, dimensions={0} | all-to-all | bytes 524288 | tf_op jit(solution)/shard_map/all_to_all | solution.py:41
  260.9 7.1 %all-to-all-start = ((bf16[8,512,128]{2,1,0:T(8,128)(2,1)}), bf16[8,512,128]{2,1,0:T(8,128)(2,1)S(1)}, u32[]{:S(2)}, u32[]{:S(2)}) async-start(bf16[8,512,128]{2,1,0:T(8,128)(2,1)} %param.8), calls=%async_computation | async-start | bytes 2097152 | tf_op jit(solution)/shard_map/all_to_all | solution.py:121
  268.0 13.7 %all-to-all-done = bf16[8,512,128]{2,1,0:T(8,128)(2,1)S(1)} async-done(((bf16[8,512,128]{2,1,0:T(8,128)(2,1)}), bf16[8,512,128]{2,1,0:T(8,128)(2,1)S(1)}, u32[]{:S(2)}, u32[]{:S(2)}) %all-to-all-start) | async-done | bytes 1048608 | tf_op jit(solution)/shard_map/all_to_all | solution.py:121
  282.4 4.1 all-to-all-start.6
  286.5 1.9 fusion.35
  288.4 11.2 %all-to-all-done.6 = f32[32,8,256]{2,1,0:T(8,128)S(1)} async-done(((f32[32,8,256]{2,1,0:T(8,128)}), f32[32,8,256]{2,1,0:T(8,128)S(1)}, u32[]{:S(2)}, u32[]{:S(2)}) %all-to-all-start.6) | async-done | bytes 262176 | tf_op jit(solution)/shard_map/all_to_all | solution.py:17
  300.0 11.7 %cholesky.164 = f32[128,128]{1,0:T(8,128)S(1)} custom-call(f32[128,128]{1,0:T(8,128)S(1)} %cholesky.197), custom_call_target="Cholesky" | custom-call | tf_op jit(solution)/shard_map/jit(cholesky)/cholesky | solution.py:116
  311.8 9.8 %custom-call.20 = f32[1,128,128]{1,2,0:T(8,128)S(1)} custom-call(f32[1,128,128]{2,1,0:T(8,128)S(1)} %get-tuple-element.45), custom_call_target="InvertDiagBlocksLowerTriangular" | custom-call | tf_op jit(solution)/shard_map/jit(cholesky)/cholesky | solution.py:116
  322.1 11.7 %cholesky.181 = f32[128,128]{1,0:T(8,128)S(1)} custom-call(f32[128,128]{1,0:T(8,128)S(1)} %convolution_subtract_fusion.4), custom_call_target="Cholesky" | custom-call | tf_op jit(solution)/shard_map/jit(cholesky)/cholesky | solution.py:116
  336.6 4.1 while.3
  337.2 1.4 bitcast_dynamic-update-slice_fusion.5
  339.3 1.4 bitcast_dynamic-update-slice_fusion.5
  340.7 19.9 %custom-call.17 = f32[2,128,128]{1,2,0:T(8,128)S(1)} custom-call(f32[2,128,128]{2,1,0:T(8,128)S(1)} %get-tuple-element.21), custom_call_target="InvertDiagBlocksLowerTriangular" | custom-call | tf_op jit(solution)/shard_map/triangular_solve | solution.py:118
  362.8 2.0 fusion.2
  364.8 16.7 %copy.57 = bf16[1,4096,128]{2,0,1:T(2,128)(2,1)S(1)} copy(bf16[1,4096,128]{2,1,0:T(8,128)(2,1)S(1)} %fusion.2) | data formatting | bytes 2097152 | tf_op jit(solution)/shard_map/broadcast_in_dim | solution.py:129
  382.1 22.4 %reduce.8 = bf16[4096,128]{1,0:T(8,128)(2,1)S(1)} reduce(bf16[4096,1,128]{2,1,0:T(2,128)(2,1)S(1)} %bitcast.142, bf16[]{:T(256)} %broadcast.130), dimensions={1}, to_apply=%bitcast.125.reduce_sub_computation | reduce | bytes 2097154
  404.5 1.1 reshape.82
  405.6 21.0 %all_to_all.53 = bf16[8,2,32768]{2,1,0:T(2,128)(2,1)S(1)} all-to-all(bf16[8,2,32768]{2,1,0:T(2,128)(2,1)} %reshape.82), channel_id=1, replica_groups=mesh['dp_0'=2,'dp_1'=8,'dp_2'=2,'blk'=8] {'blk'}, dimensions={0} | all-to-all | bytes 2097152 | tf_op jit(solution)/shard_map/all_to_all | solution.py:129
  426.6 3.5 reshape.83
  430.0 2.7 copy.43
  (64 shorter events, 11.6 us)
Async XLA Ops:
  0.0 6.0 %copy-start = (bf16[1,4096,256]{2,1,0:T(8,128)(2,1)S(1)}, bf16[1,4096,256]{2,1,0:T(8,128)(2,1)}, u32[]{:S(2)}) copy-start(bf16[1,4096,256]{2,1,0:T(8,128)(2,1)} %param.7) | copy-start | bytes 6291460
  0.0 6.0 %copy-start.3 = (bf16[1,512,4096]{2,1,0:T(8,128)(2,1)S(1)}, bf16[1,512,4096]{2,1,0:T(8,128)(2,1)}, u32[]{:S(2)}) copy-start(bf16[1,512,4096]{2,1,0:T(8,128)(2,1)} %param.5) | copy-start | bytes 12582916
  24.2 10.1 %all-to-all-start.1 = ((f32[2,16,128,256]{2,1,3,0:T(8,128)}), f32[2,16,128,256]{2,1,3,0:T(8,128)}, u32[]{:S(2)}, u32[]{:S(2)}) async-start(f32[2,16,128,256]{2,1,3,0:T(8,128)} %bitcast.138), calls=%async_computation.1 | async-start | bytes 8388608 | tf_op jit(solution)/shard_map/all_to_all | solution.py:41
  98.3 53.7 %all-to-all-start.3 = ((f32[16,128,256]{2,1,0:T(8,128)}), f32[16,128,256]{2,1,0:T(8,128)S(1)}, u32[]{:S(2)}, u32[]{:S(2)}) async-start(f32[16,128,256]{2,1,0:T(8,128)} %broadcast_in_dim.8), calls=%async_computation.3 | async-start | bytes 4194304 | tf_op jit(solution)/shard_map/all_to_all | solution.py:17
  159.6 1.9 copy-start.2
  233.4 5.6 %copy-start.7 = (bf16[4096,128]{0,1:T(8,128)(2,1)}, bf16[4096,128]{0,1:T(8,128)(2,1)S(1)}, u32[]{:S(2)}) copy-start(bf16[4096,128]{0,1:T(8,128)(2,1)S(1)} %get-tuple-element.52) | copy-start | bytes 3145732
  233.4 6.6 %copy-start.4 = (bf16[1,512,4096]{2,1,0:T(8,128)(2,1)S(1)}, bf16[1,512,4096]{2,1,0:T(8,128)(2,1)}, u32[]{:S(2)}) copy-start(bf16[1,512,4096]{2,1,0:T(8,128)(2,1)} %param.5) | copy-start | bytes 12582916
  239.0 1.0 copy-start.5
  241.2 45.3 %copy-start.6 = (bf16[4096,128]{0,1:T(8,128)(2,1)S(1)}, bf16[4096,128]{0,1:T(8,128)(2,1)}, u32[]{:S(2)}) copy-start(bf16[4096,128]{0,1:T(8,128)(2,1)} %copy-done.5) | copy-start | bytes 3145732
  260.9 20.8 %all-to-all-start = ((bf16[8,512,128]{2,1,0:T(8,128)(2,1)}), bf16[8,512,128]{2,1,0:T(8,128)(2,1)S(1)}, u32[]{:S(2)}, u32[]{:S(2)}) async-start(bf16[8,512,128]{2,1,0:T(8,128)(2,1)} %param.8), calls=%async_computation | async-start | bytes 2097152 | tf_op jit(solution)/shard_map/all_to_all | solution.py:121
  282.4 17.3 %all-to-all-start.6 = ((f32[32,8,256]{2,1,0:T(8,128)}), f32[32,8,256]{2,1,0:T(8,128)S(1)}, u32[]{:S(2)}, u32[]{:S(2)}) async-start(f32[32,8,256]{2,1,0:T(8,128)} %broadcast_in_dim.11), calls=%async_computation.6 | async-start | bytes 524288 | tf_op jit(solution)/shard_map/all_to_all | solution.py:17
  404.5 28.3 %copy-start.1 = (bf16[1,4096,256]{2,1,0:T(8,128)(2,1)S(1)}, bf16[1,4096,256]{2,1,0:T(8,128)(2,1)}, u32[]{:S(2)}) copy-start(bf16[1,4096,256]{2,1,0:T(8,128)(2,1)} %param.7) | copy-start | bytes 6291460
where the time goes:
time: 441 us; the launch traced here: 433 us
  other arithmetic  134 us (30%)
  blocking collectives  106 us (24%)
  waiting for transfers between devices  78.3 us (18%)
  local copies, waits for them, and re-layouts  53.2 us (12%)
  matrix products  36.3 us (8%)
  starting transfers between devices  21.6 us (5%)
    all_to_all x2, waiting for transfers between devices, copy_for_each(): lax.all_to_all(jnp.broadcast_to(x[None], (devices, *x.shape)), axis, 0, 0...  60.2 us
    all_to_all x1, blocking collectives, sum_by_axis(): lax.all_to_all(nearer, far, split_axis=0, concat_axis=0, tiled=True)  58.8 us
    another operation x7, other arithmetic, shards(): lower_factor = jnp.linalg.cholesky(shifted)  34.7 us
    another operation x6, other arithmetic, cholesky_pass(): lower_factor = jnp.linalg.cholesky(gram_matrix)  34.4 us
    unnamed x1, other arithmetic  22.4 us
    all_to_all x1, blocking collectives, shards(): lax.all_to_all(fresh[None], 'blk', split_axis=1, concat_axis=0, tiled=True)  21 us
    another operation x2, other arithmetic, shards(): lax.linalg.triangular_solve(lower_factor, half_solved, left_side=True, lo...  20 us
    another operation x3, other arithmetic, cholesky_pass(): lax.linalg.triangular_solve(lower_factor, columns, left_side=False, lower...  19.9 us
  transfers between devices with their start and end apart: 4, of which 4 were waited for; matrix products, arithmetic and copies ran while one was open for 0% of the time, Pallas kernels for 0%

commit v1 on v0

v1 whole, which is shorter than its diff:
```python
import jax
import jax.numpy as jnp
from jax import lax
from jax.sharding import PartitionSpec as P


def inner_gram(columns):
    return lax.dot_general(
        columns, columns, (((0,), (0,)), ((), ())), precision=lax.Precision.HIGHEST
    )


def cholesky_pass(columns, gram_matrix):
    lower_factor = jnp.linalg.cholesky(gram_matrix)
    return lax.linalg.triangular_solve(
        lower_factor, columns, left_side=False, lower=True, transpose_a=True
    )


def shards(inputs, out_grads, test_matrix, momentum):
    features = inputs[0]
    errors = out_grads[0]
    probes = test_matrix[0]
    replicas = lax.axis_size("dp")
    scale = 1.0 / (features.shape[1] * features.shape[0] * replicas)
    columns = lax.all_to_all(momentum, "blk", split_axis=0, concat_axis=1, tiled=True)[0]
    projected = jnp.dot(features, probes, preferred_element_type=jnp.float32).astype(jnp.bfloat16)
    token_gram = lax.dot_general(
        errors, errors, (((1,), (1,)), ((), ())), preferred_element_type=jnp.float32
    ).astype(jnp.bfloat16)
    mixed_rows = jnp.dot(token_gram, projected, preferred_element_type=jnp.float32).astype(
        jnp.bfloat16
    )
    sketch_term = (
        lax.dot_general(
            features, mixed_rows, (((0,), (0,)), ((), ())), preferred_element_type=jnp.float32
        )
        * scale
    )
    sketch = lax.psum(sketch_term, "dp")
    basis = cholesky_pass(sketch, inner_gram(sketch)).astype(jnp.bfloat16)
    reduced = jnp.dot(features, basis, preferred_element_type=jnp.float32).astype(jnp.bfloat16)
    shaped = jnp.dot(token_gram, reduced, preferred_element_type=jnp.float32).astype(jnp.bfloat16)
    core_term = (
        lax.dot_general(
            reduced, shaped, (((0,), (0,)), ((), ())), preferred_element_type=jnp.float32
        )
        * scale
    )
    core_matrix = lax.psum(core_term, "dp")
    shifted = core_matrix + jnp.eye(core_matrix.shape[0], dtype=jnp.float32)
    lower_factor = jnp.linalg.cholesky(shifted)
    half_solved = lax.linalg.triangular_solve(lower_factor, core_matrix, left_side=True, lower=True)
    factor = lax.linalg.triangular_solve(
        lower_factor, half_solved, left_side=True, lower=True, transpose_a=True
    )
    coeffs = lax.dot_general(
        basis, columns, (((0,), (0,)), ((), ())), preferred_element_type=jnp.float32
    )
    scaled = jnp.dot(factor, coeffs, precision=lax.Precision.HIGHEST).astype(jnp.bfloat16)
    fresh = (
        columns.astype(jnp.float32) - jnp.dot(basis, scaled, preferred_element_type=jnp.float32)
    ).astype(jnp.bfloat16)
    return lax.all_to_all(fresh[None], "blk", split_axis=1, concat_axis=0, tiled=True)


def solution(mesh):
    in_specs = (P("blk", "dp", None), P("blk", "dp", None), P("blk", None, None), P(None, "blk", "dp"))
    out_specs = P(None, "blk", "dp")
    return jax.shard_map(
        shards, mesh=mesh, in_specs=in_specs, out_specs=out_specs, check_vma=False
    )
```

time: 441 us -> 713 us (1.62)
  waiting for transfers between devices: 78.3 us -> 447 us
  blocking collectives: 106 us -> 22.7 us
  local copies, waits for them, and re-layouts: 53.2 us -> 34.1 us
  starting transfers between devices: 21.6 us -> 7.39 us
  between operations: 3.54 us -> 16.7 us
  matrix products: 36.3 us -> 44.2 us
    psum x0 -> x2, waiting for transfers between devices: none -> 447 us  [the longest x1 230 us: shards(): sketch = lax.psum(sketch_term, 'dp')]
    all_to_all x3 -> x0, blocking collectives: 84.9 us -> none  [the longest x1 58.8 us: sum_by_axis(): lax.all_to_all(nearer, far, split_axis=0, concat_axis=0, tiled=True)]
    all_to_all x3 -> x0, waiting for transfers between devices: 64.6 us -> none  [the longest x2 60.2 us: copy_for_each(): lax.all_to_all(jnp.broadcast_to(x[None], (devices, *x.shape)), axis, 0, 0...]
    all_to_all x3 -> x0, starting transfers between devices: 14.5 us -> none  [the longest x2 8.88 us: copy_for_each(): lax.all_to_all(jnp.broadcast_to(x[None], (devices, *x.shape)), axis, 0, 0...]
    all_to_all x1, waiting for transfers between devices: 13.7 us -> 0.01 us  [shards(): lax.all_to_all(momentum, 'blk', split_axis=0, concat_axis=1, tiled=True)[0]]
    another operation x14 -> x12, local copies, waits for them, and re-layouts: 19.1 us -> 7.62 us  [the longest x2 11.1 us: in_blocks(): x.reshape(*lengths[:dim], devices, lengths[dim] // devices, *lengths[dim...]
  transfers between devices with their start and end apart: 4 -> 3, of which waited for: 4 -> 2; matrix products, arithmetic and copies ran while one was open for 0% -> 12% of each run, Pallas kernels for 0% -> 0%
where the time goes in v1:
time: 713 us; the launch traced here: 706 us
  waiting for transfers between devices  447 us (63%)
  other arithmetic  134 us (19%)
  matrix products  44.2 us (6%)
  local copies, waits for them, and re-layouts  34.1 us (5%)
  blocking collectives  22.7 us (3%)
  between operations  16.7 us (2%)
  starting transfers between devices  7.39 us (1%)
    psum x1, waiting for transfers between devices, shards(): sketch = lax.psum(sketch_term, 'dp')  230 us
    psum x1, waiting for transfers between devices, shards(): core_matrix = lax.psum(core_term, 'dp')  216 us
    another operation x7, other arithmetic, shards(): lower_factor = jnp.linalg.cholesky(shifted)  34.8 us
    another operation x6, other arithmetic, cholesky_pass(): lower_factor = jnp.linalg.cholesky(gram_matrix)  34 us
    unnamed x1, other arithmetic  23.4 us
    all_to_all x1, blocking collectives, shards(): lax.all_to_all(fresh[None], 'blk', split_axis=1, concat_axis=0, tiled=True)  22.7 us
    another operation x3, other arithmetic, cholesky_pass(): lax.linalg.triangular_solve(lower_factor, columns, left_side=False, lower...  19.9 us
    another operation x2, other arithmetic, shards(): lax.linalg.triangular_solve(lower_factor, half_solved, left_side=True, lo...  19.7 us
  transfers between devices with their start and end apart: 3, of which 2 were waited for; matrix products, arithmetic and copies ran while one was open for 12% of the time, Pallas kernels for 0%

profile of v1, /device:TPU:8, one launch (start us, length us, event | category | flops | bytes accessed | tf_op | source)
XLA Modules:
  0.0 705.7 jit_solution(12601974615667945552)
XLA Ops:
  6.5 6.0 fusion.13
  12.5 1.3 fusion.16
  13.8 5.9 fusion
  19.7 7.4 %all-to-all-start = ((bf16[8,512,128]{2,1,0:T(8,128)(2,1)}), bf16[8,512,128]{2,1,0:T(8,128)(2,1)}, u32[]{:S(2)}, u32[]{:S(2)}) async-start(bf16[8,512,128]{2,1,0:T(8,128)(2,1)} %param.8), calls=%async_computation | async-start | bytes 2097152 | tf_op jit(solution)/shard_map/all_to_all | solution.py:26
  27.1 230.4 %all-reduce.4.cloned.1.call-done = f32[4096,256]{0,1:T(8,128)} async-done(((f32[4096,256]{0,1:T(8,128)}), f32[4096,256]{0,1:T(8,128)}) %all-reduce.4.cloned.1.call-update) | async-done | bytes 4194320 | tf_op jit(solution)/shard_map/psum | solution.py:40
  257.5 12.4 %fusion.53 = f32[256,256]{1,0:T(8,128)S(1)} fusion(f32[4096,256]{0,1:T(8,128)} %all-reduce.4.cloned.1.call-done), kind=kOutput, calls=%fused_computation.90 | convolution fusion | flops 3221225472 | bytes 4456448 | tf_op jit(solution)/shard_map/dot_general | solution.py:8
  270.1 11.7 %cholesky.130 = f32[128,128]{1,0:T(8,128)S(1)} custom-call(f32[128,128]{1,0:T(8,128)S(1)} %cholesky.194), custom_call_target="Cholesky" | custom-call | tf_op jit(solution)/shard_map/jit(cholesky)/cholesky | solution.py:14
  281.9 9.8 %custom-call.19 = f32[1,128,128]{1,2,0:T(8,128)S(1)} custom-call(f32[1,128,128]{2,1,0:T(8,128)S(1)} %get-tuple-element.49), custom_call_target="InvertDiagBlocksLowerTriangular" | custom-call | tf_op jit(solution)/shard_map/jit(cholesky)/cholesky | solution.py:14
  292.2 11.7 %cholesky.147 = f32[128,128]{1,0:T(8,128)S(1)} custom-call(f32[128,128]{1,0:T(8,128)S(1)} %convolution_subtract_fusion.5), custom_call_target="Cholesky" | custom-call | tf_op jit(solution)/shard_map/jit(cholesky)/cholesky | solution.py:14
  303.9 0.7 compare_reduce_fusion.2
  306.0 3.9 while.2
  306.0 0.6 fusion.77
  306.6 1.3 bitcast_dynamic-update-slice_fusion.4
  307.9 0.6 fusion.77
  308.5 1.3 bitcast_dynamic-update-slice_fusion.4
  309.8 19.8 %custom-call.16 = f32[2,128,128]{1,2,0:T(8,128)S(1)} custom-call(f32[2,128,128]{2,1,0:T(8,128)S(1)} %get-tuple-element.13), custom_call_target="InvertDiagBlocksLowerTriangular" | custom-call | tf_op jit(solution)/shard_map/triangular_solve | solution.py:15
  329.7 3.7 fusion.52
  333.5 2.0 convolution_subtract_fusion.1
  335.5 2.0 convolution_convert_fusion
  337.5 1.0 copy-done.5
  338.5 1.3 fusion.21
  339.8 1.3 fusion.25
  341.1 2.6 fusion.26
  343.7 216.2 %all-reduce.6.cloned.1.call-done = f32[256,256]{0,1:T(8,128)} async-done(((f32[256,256]{0,1:T(8,128)}), f32[256,256]{0,1:T(8,128)}) %all-reduce.6.cloned.1.call-update) | async-done | bytes 262160 | tf_op jit(solution)/shard_map/psum | solution.py:50
  560.0 1.0 convert_add_fusion
  561.1 1.0 fusion.30
  562.1 11.9 %cholesky.164 = f32[128,128]{1,0:T(8,128)S(1)} custom-call(f32[128,128]{1,0:T(8,128)S(1)} %cholesky.197), custom_call_target="Cholesky" | custom-call | tf_op jit(solution)/shard_map/jit(cholesky)/cholesky | solution.py:52
  574.1 9.8 %custom-call.20 = f32[1,128,128]{1,2,0:T(8,128)S(1)} custom-call(f32[1,128,128]{2,1,0:T(8,128)S(1)} %get-tuple-element.45), custom_call_target="InvertDiagBlocksLowerTriangular" | custom-call | tf_op jit(solution)/shard_map/jit(cholesky)/cholesky | solution.py:52
  584.4 11.7 %cholesky.181 = f32[128,128]{1,0:T(8,128)S(1)} custom-call(f32[128,128]{1,0:T(8,128)S(1)} %convolution_subtract_fusion.4), custom_call_target="Cholesky" | custom-call | tf_op jit(solution)/shard_map/jit(cholesky)/cholesky | solution.py:52
  596.2 0.7 compare_reduce_fusion
  596.9 0.6 compare_reduce_fusion.1
  598.7 3.8 while.3
  598.8 0.6 fusion.78
  599.4 1.3 bitcast_dynamic-update-slice_fusion.5
  600.7 0.6 fusion.78
  601.3 1.3 bitcast_dynamic-update-slice_fusion.5
  602.6 19.7 %custom-call.17 = f32[2,128,128]{1,2,0:T(8,128)S(1)} custom-call(f32[2,128,128]{2,1,0:T(8,128)S(1)} %get-tuple-element.21), custom_call_target="InvertDiagBlocksLowerTriangular" | custom-call | tf_op jit(solution)/shard_map/triangular_solve | solution.py:54
  622.3 0.3 fusion.32
  622.6 0.4 convolution_subtract_fusion.3
  624.2 0.4 convolution_convert_fusion.3
  624.6 2.7 fusion.2
  627.2 17.3 %copy.23 = bf16[1,4096,128]{2,0,1:T(2,128)(2,1)} copy(bf16[1,4096,128]{2,1,0:T(8,128)(2,1)S(1)} %fusion.2) | data formatting | bytes 2097152 | tf_op jit(solution)/shard_map/broadcast_in_dim | solution.py:64
  644.5 0.5 broadcast.127
  645.0 23.4 %reduce.8 = bf16[4096,128]{1,0:T(8,128)(2,1)S(1)} reduce(bf16[4096,1,128]{2,1,0:T(2,128)(2,1)} %bitcast.111, bf16[]{:T(256)} %broadcast.127), dimensions={1}, to_apply=%bitcast.97.reduce_sub_computation | reduce | bytes 2097154
  668.5 1.1 reshape.68
  669.6 22.7 %all_to_all.21 = bf16[8,2,32768]{2,1,0:T(2,128)(2,1)S(1)} all-to-all(bf16[8,2,32768]{2,1,0:T(2,128)(2,1)} %reshape.68), channel_id=1, replica_groups=mesh['dp'=32,'blk'=8] {'blk'}, dimensions={0} | all-to-all | bytes 2097152 | tf_op jit(solution)/shard_map/all_to_all | solution.py:64
  692.3 3.5 reshape.69
  695.7 2.7 copy.21
  (47 shorter events, 2.8 us)
Async XLA Ops:
  6.5 6.0 copy-start
  6.5 251.0 %all-reduce.4.cloned.1.call-start = ((), (), s32[]{:S(2)}) async-start(), calls=%async_computation.2 | async-start | bytes 8388608 | tf_op jit(solution)/shard_map/psum | solution.py:40
  6.5 6.0 copy-start.2
  19.7 321.4 %all-to-all-start = ((bf16[8,512,128]{2,1,0:T(8,128)(2,1)}), bf16[8,512,128]{2,1,0:T(8,128)(2,1)}, u32[]{:S(2)}, u32[]{:S(2)}) async-start(bf16[8,512,128]{2,1,0:T(8,128)(2,1)} %param.8), calls=%async_computation | async-start | bytes 2097152 | tf_op jit(solution)/shard_map/all_to_all | solution.py:26
  27.1 532.8 %all-reduce.6.cloned.1.call-start = ((), (), s32[]{:S(2)}) async-start(), calls=%async_computation.3 | async-start | bytes 524288 | tf_op jit(solution)/shard_map/psum | solution.py:50
  329.7 3.8 copy-start.1
  333.5 4.1 copy-start.6
  333.5 5.0 copy-start.3
  337.5 1.0 copy-start.5
  560.0 62.3 %copy-start.4 = (f32[256,256]{0,1:T(8,128)S(1)}, f32[256,256]{0,1:T(8,128)}, u32[]{:S(2)}) copy-start(f32[256,256]{0,1:T(8,128)} %all-reduce.6.cloned.1.call-done) | copy-start | bytes 786436
Sparse Core Ops, SparseCore 0:
  19.9 237.6 all-reduce.3
  341.2 218.6 all-reduce.5
